TPU v7x, 32 devices: a whole 2x2x4 slice. The times are simulated.
32 devices in a mesh: groups: 2 (over y), ctx: 4 (over z), head: 4 (over x, core).
Axes of the slice: x: 2, y: 2, z: 4, core: 2. Of those that a mesh axis runs over, the one named last changes fastest.
Arguments:
- queries: bfloat16 [8192, 512], P(('groups', 'ctx', 'head')), parts along dimension 0, may hold values from -8 to 8, as said below
- keys: bfloat16 [8192, 512], P(('groups', 'ctx', 'head')), parts along dimension 0, may hold values from -8 to 8
- values: bfloat16 [8192, 4096], P(('groups', 'ctx', 'head')), parts along dimension 0, may hold values from -6 to 6
- gain: float32 [4096], P('head'), may hold values from 0.5 to 1.5
Outputs:
- mixed: bfloat16 [8192, 4096], P(('groups', 'ctx', 'head')), parts along dimension 0
There are 2 independent parts, one for each index of `groups`. A program takes and returns all parts, laid end to end along the dimension named above; an argument that names none is the same for every part. Nothing has to cross between parts.
Inputs may be any that keep to these rules, and one draw needn't show every extreme that they name: `queries`: query entries lie in the stated range.
All inputs are finite; a program needn't handle non-finite values.
Results may differ from a plain program's by a relative error of at most 0.0054.
Values may be sent and summed in bfloat16 or wider, within the bound.
No kernel may reach another device: no remote copies, remote signals or barrier semaphores. Data moves between devices by JAX's collectives and lax.ppermute only.
A program may use at most 128 MiB of HBM per device.

v0:
```python
import math
import jax
import jax.numpy as jnp
from jax import lax
from jax.sharding import PartitionSpec as P

HEADS = 32
KD = 16
VD = 128
WINDOW = 64
outer_scale = 1.0 / (4.0 * math.sqrt(2.0))
epsilon = 1e-06


def shifted(shard, axis, by):
    peers = lax.axis_size(axis)
    pairs = [(i, i + by) for i in range(peers) if 0 <= i + by < peers]
    return lax.ppermute(shard, axis, pairs)


def entering(shard, axis, combine, identity):
    peers, here = (lax.axis_size(axis), lax.axis_index(axis))
    everything = lax.all_gather(shard, axis)
    start = jnp.broadcast_to(jnp.asarray(identity, shard.dtype), shard.shape)

    def hop(k, before):
        reached = k < here
        new = combine(before, everything[k])
        return jnp.where(reached, new, before)

    return lax.fori_loop(0, peers, hop, start)


def feature_map(vector):
    width = vector.shape[-1]
    products = (vector[..., :, None] * vector[..., None, :]).reshape(
        vector.shape[:-1] + (width * width,)
    )
    unit_column = jnp.ones(vector.shape[:-1] + (1,), jnp.float32)
    return jnp.concatenate([unit_column, vector * 0.5, products * outer_scale], axis=-1)


def per_device(queries, keys, values, gain):
    local_tokens = queries.shape[0]
    query_tok = queries.reshape(local_tokens, HEADS, KD)
    key_tok = keys.reshape(local_tokens, HEADS, KD)
    value_tok = values.reshape(local_tokens, HEADS, VD)
    query_head, key_head, value_head = (
        lax.all_to_all(query_tok, "head", split_axis=1, concat_axis=0, tiled=True),
        lax.all_to_all(key_tok, "head", split_axis=1, concat_axis=0, tiled=True),
        lax.all_to_all(value_tok, "head", split_axis=1, concat_axis=0, tiled=True),
    )
    span_rows = query_head.shape[0]
    heads_here = query_head.shape[1]
    block_rows = min(512, span_rows)
    block_count = span_rows // block_rows
    tail_keys, tail_values = shifted(
        (key_head[span_rows - WINDOW :], value_head[span_rows - WINDOW :]), "ctx", 1
    )
    key_ext = jnp.concatenate([tail_keys, key_head], axis=0)
    value_ext = jnp.concatenate([tail_values, value_head], axis=0)
    first_span = lax.axis_index("ctx") == 0
    key_features = feature_map(key_head.astype(jnp.float32)).astype(jnp.bfloat16)
    own_state = jnp.einsum(
        "bhf,bhv->hfv", key_features, value_head, preferred_element_type=jnp.float32
    )

    def combine_states(earlier, later):
        return earlier + later

    prefix = entering(own_state, "ctx", combine_states, jnp.zeros_like(own_state))

    def block_step(state, block_index):
        start = block_index * block_rows
        query_block = lax.dynamic_slice_in_dim(query_head, start, block_rows, 0)
        key_block = lax.dynamic_slice_in_dim(key_head, start, block_rows, 0)
        value_block = lax.dynamic_slice_in_dim(value_head, start, block_rows, 0)
        key_feat = lax.dynamic_slice_in_dim(key_features, start, block_rows, 0)
        key_window = lax.dynamic_slice_in_dim(key_ext, start, block_rows + WINDOW, 0)
        value_window = lax.dynamic_slice_in_dim(value_ext, start, block_rows + WINDOW, 0)
        scores = (
            jnp.einsum("bhd,chd->hbc", query_block, key_block, preferred_element_type=jnp.float32)
            * 0.25
        )
        row_pos = jnp.arange(block_rows)[:, None]
        col_pos = jnp.arange(block_rows)[None, :]
        kernel = jnp.where(col_pos <= row_pos, 1.0 + scores + 0.5 * scores * scores, 0.0).astype(
            jnp.bfloat16
        )
        intra = jnp.einsum("hbc,chv->bhv", kernel, value_block, preferred_element_type=jnp.float32)
        query_feat = feature_map(query_block.astype(jnp.float32)).astype(jnp.bfloat16)
        inter = jnp.einsum(
            "bhf,hfv->bhv",
            query_feat,
            state.astype(jnp.bfloat16),
            preferred_element_type=jnp.float32,
        )
        state = state + jnp.einsum(
            "bhf,bhv->hfv", key_feat, value_block, preferred_element_type=jnp.float32
        )
        window_scores = (
            jnp.einsum("bhd,chd->hbc", query_block, key_window, preferred_element_type=jnp.float32)
            * 0.25
        )
        key_pos = jnp.arange(block_rows + WINDOW)[None, :] - WINDOW
        valid = (
            (key_pos <= row_pos)
            & (key_pos > row_pos - WINDOW)
            & ((start + key_pos >= 0) | jnp.logical_not(first_span))
        )
        masked = jnp.where(valid, window_scores, -jnp.inf)
        highest_score = jnp.max(masked, axis=2, keepdims=True)
        expo = jnp.where(valid, jnp.exp(window_scores - highest_score), 0.0)
        weights = (expo / jnp.sum(expo, axis=2, keepdims=True)).astype(jnp.bfloat16)
        window_out = jnp.einsum(
            "hbc,chv->bhv", weights, value_window, preferred_element_type=jnp.float32
        )
        return (state, (intra + inter, window_out))

    final_state, (linear_all, window_all) = lax.scan(block_step, prefix, jnp.arange(block_count))
    linear = linear_all.reshape(span_rows, heads_here, VD)
    window = window_all.reshape(span_rows, heads_here, VD)
    scale = lax.rsqrt(jnp.mean(linear * linear, axis=2, keepdims=True) + epsilon)
    gains = gain.reshape(heads_here, VD)
    mixed = (linear * scale * gains + window).astype(jnp.bfloat16)
    tokens_back = lax.all_to_all(mixed, "head", split_axis=0, concat_axis=1, tiled=True)
    return tokens_back.reshape(tokens_back.shape[0], HEADS * VD)


def solution(mesh):
    placed = (
        P(("groups", "ctx", "head"), None),
        P(("groups", "ctx", "head"), None),
        P(("groups", "ctx", "head"), None),
        P("head"),
    )
    return jax.shard_map(
        per_device,
        mesh=mesh,
        in_specs=placed,
        out_specs=P(("groups", "ctx", "head"), None),
        check_vma=False,
    )
```

profile of v0, /device:TPU:0, one launch (start us, length us, event | category | flops | bytes accessed | tf_op | source)
XLA Modules:
  0.0 278.9 jit_solution(16457745592861958230)
XLA Ops:
  8.3 4.2 %all-to-all-start = ((bf16[256,32,16]{0,2,1:T(8,128)(2,1)}), bf16[256,32,16]{0,2,1:T(8,128)(2,1)S(1)}, u32[]{:S(2)}, u32[]{:S(2)}) async-start(bf16[256,32,16]{0,2,1:T(8,128)(2,1)} %bitcast.7), calls=%async_computation | async-start | bytes 524288 | tf_op jit(solution)/shard_map/all_to_all | solution.py:50
  12.5 3.3 %copy.44 = bf16[256,4096]{0,1:T(8,128)(2,1)S(1)} copy(bf16[256,4096]{1,0:T(8,128)(2,1)} %param.10) | data formatting | bytes 4194304 | tf_op args[2]
  15.8 2.9 %copy.45 = bf16[256,32,128]{2,0,1:T(8,128)(2,1)} copy(bf16[256,32,128]{0,2,1:T(8,128)(2,1)S(1)} %bitcast.80) | data formatting | bytes 4194304 | tf_op jit(solution)/shard_map/reshape | solution.py:47
  18.7 3.6 %all-to-all-start.1 = ((bf16[256,32,128]{2,0,1:T(8,128)(2,1)}), bf16[256,32,128]{2,0,1:T(8,128)(2,1)S(1)}, u32[]{:S(2)}, u32[]{:S(2)}) async-start(bf16[256,32,128]{2,0,1:T(8,128)(2,1)} %copy.45), calls=%async_computation.1 | async-start | bytes 4194304 | tf_op jit(solution)/shard_map/all_to_all | solution.py:51
  23.8 3.9 %pad_maximum_fusion = bf16[1024,8,273]{0,2,1:T(8,128)(2,1)} fusion(bf16[1024,8,256]{0,2,1:T(8,128)(2,1)S(1)} %bitcast.76, bf16[1024,8,16]{0,2,1:T(8,128)(2,1)S(1)} %multiply_convert_fusion.3, bf16[273]{0:T(512)(128)(2,1)S(1)} %pad.7.clone), kind=kLoop, calls=%fused_computation.66 | loop fusion | flops 13418496 | bytes 8929826 | tf_op jit(solution)/shard_map/concatenate | solution.py:40
  27.7 20.3 %all-to-all-done.1 = bf16[256,32,128]{2,0,1:T(8,128)(2,1)S(1)} async-done(((bf16[256,32,128]{2,0,1:T(8,128)(2,1)}), bf16[256,32,128]{2,0,1:T(8,128)(2,1)S(1)}, u32[]{:S(2)}, u32[]{:S(2)}) %all-to-all-start.1) | async-done | bytes 2097184 | tf_op jit(solution)/shard_map/all_to_all | solution.py:51
  49.4 4.4 %fusion.77 = f32[8,273,128]{2,1,0:T(8,128)S(1)} fusion(bf16[1024,8,273]{0,2,1:T(8,128)(2,1)} %pad_maximum_fusion, bf16[1024,8,128]{2,0,1:T(8,128)(2,1)} %bitcast.15), kind=kOutput, calls=%fused_computation.77 | convolution fusion | flops 572522496 | bytes 7688192 | tf_op jit(solution)/shard_map/bhf,bhv->hfv/dot_general | solution.py:64
  55.9 3.4 %all-to-all-start.2 = ((bf16[256,32,16]{0,2,1:T(8,128)(2,1)}), bf16[256,32,16]{0,2,1:T(8,128)(2,1)S(1)}, u32[]{:S(2)}, u32[]{:S(2)}) async-start(bf16[256,32,16]{0,2,1:T(8,128)(2,1)} %bitcast.17), calls=%async_computation.2 | async-start | bytes 524288 | tf_op jit(solution)/shard_map/all_to_all | solution.py:49
  59.4 4.1 %collective-permute-start.1 = (bf16[64,8,16]{0,2,1:T(8,128)(2,1)S(1)}, bf16[64,8,16]{0,2,1:T(8,128)(2,1)S(1)}, u32[]{:S(2)}, u32[]{:S(2)}) collective-permute-start(bf16[64,8,16]{0,2,1:T(8,128)(2,1)S(1)} %slice.9), channel_id=1, source_target_pairs={{0,4},{4,8},{8,12},{1,5},{5,9},{9,13},{2,6},{6,10},{10,14},{3,7},{... | collective-permute-start | bytes 49160 | tf_op jit(solution)/shard_map/ppermute | solution.py:18
  67.0 4.3 %collective-permute-start = (bf16[64,8,128]{2,0,1:T(8,128)(2,1)S(1)}, bf16[64,8,128]{2,0,1:T(8,128)(2,1)S(1)}, u32[]{:S(2)}, u32[]{:S(2)}) collective-permute-start(bf16[64,8,128]{2,0,1:T(8,128)(2,1)S(1)} %slice.8), channel_id=1, source_target_pairs={{0,4},{4,8},{8,12},{1,5},{5,9},{9,13},{2,6},{6,10},{10,14},{3,7},{... | collective-permute-start | bytes 393224 | tf_op jit(solution)/shard_map/ppermute | solution.py:18
  72.2 5.1 %collective-permute-done = bf16[64,8,128]{2,0,1:T(8,128)(2,1)S(1)} collective-permute-done((bf16[64,8,128]{2,0,1:T(8,128)(2,1)S(1)}, bf16[64,8,128]{2,0,1:T(8,128)(2,1)S(1)}, u32[]{:S(2)}, u32[]{:S(2)}) %collective-permute-start) | collective-permute-done | bytes 131104 | tf_op jit(solution)/shard_map/ppermute | solution.py:18
  77.4 3.1 %pad_maximum_fusion.1 = bf16[1088,8,128]{2,0,1:T(8,128)(2,1)} fusion(bf16[1024,8,128]{2,0,1:T(8,128)(2,1)} %bitcast.15, bf16[64,8,128]{2,0,1:T(8,128)(2,1)S(1)} %collective-permute-done), kind=kLoop, calls=%fused_computation.72 | loop fusion | flops 4456448 | bytes 4456448 | tf_op jit(solution)/shard_map/concatenate | solution.py:61
  80.5 65.2 %all-gather.3.cloned.1.call-done = f32[32,273,128]{2,0,1:T(8,128)} async-done(((f32[8,273,128]{2,0,1:T(8,128)}), f32[32,273,128]{2,0,1:T(8,128)}) %all-gather.3.cloned.1.call-update) | async-done | bytes 4472848 | tf_op jit(solution)/shard_map/all_gather | solution.py:23
  145.7 7.5 %while.32 = (s32[]{:T(128)}, f32[8,273,128]{2,1,0:T(8,128)S(1)}, s32[]{:T(128)}, f32[4,8,273,128]{3,1,0,2:T(8,128)}, s32[]{:T(128)}, /*index=5*/s32[]{:T(128)}) while((s32[]{:T(128)}, f32[8,273,128]{2,1,0:T(8,128)S(1)}, s32[]{:T(128)}, f32[4,8,273,128]{3,1,0,2:T(8,128)}, s32[]{:T(128)}, /*index=5*/s32[]{:T(128)}) %tuple.69), condition=%wide.region_1.2_spmd.clone, body=%wide.region_0.1_spmd.clone.sunk | while | flops 838660 | bytes 5591141 | solution.py:31
  153.2 71.0 %while.31 = (s32[]{:T(128)}, f32[8,273,128]{2,1,0:T(8,128)S(1)}, f32[2,512,8,128]{1,3,2,0:T(8,128)}, f32[2,512,8,128]{3,2,1,0:T(8,128)}, s32[2]{0:T(128)S(1)}, /...) while((s32[]{:T(128)}, f32[8,273,128]{2,1,0:T(8,128)S(1)}, ...), condition=%wide.region_5.6_spmd, body=%wide.region_2.5_spmd.sunk | while | flops 1977677568 | bytes 70311560 | solution.py:120
  158.9 4.5 %fusion.111 = f32[8,128,512]{2,1,0:T(8,128)S(1)} fusion(pred[512,512]{1,0:T(8,128)(4,1)} %iota_compare_fusion.3, bf16[1024,8,128]{2,0,1:T(8,128)(2,1)} %get-tuple-element.495, s32[]{:T(128)S(6)} %select_n.84, bf16[1024,8,16]{0,2,1:T(8,128)(2,1)} %copy-done.1, bf16[1024,8,16]{0,2,1:T(8,128)(2,1)} %get-tuple-element.496), kind=kOutput, calls=%fused_computation.12.clone.1 | convolution fusion | flops 618659840 | bytes 3671552 | tf_op jit(solution)/shard_map/while/body/eval_jaxpr/hbc,chv->bhv/dot_general | solution.py:90
  164.2 3.7 %bitcast_dynamic-update-slice_fusion.2 = f32[2,512,8,128]{1,3,2,0:T(8,128)} fusion(f32[2,512,8,128]{1,3,2,0:T(8,128)} %get-tuple-element.472, s32[]{:T(128)S(6)} %copy.85, f32[8,128,512]{2,1,0:T(8,128)S(1)} %fusion.111, bf16[512,8,256]{0,2,1:T(8,128)(2,1)S(1)} %bitcast.73, bf16[512,8,16]{0,2,1:T(8,128)(2,1)} %multiply_convert_fusion.7, ...), kind=kOutput, calls=%fused_computation.22.clone.1 | convolution fusion | flops 293774336 | bytes 7541286 | tf_op jit(solution)/shard_map/while/body/eval_jaxpr/bhf,hfv->bhv/dot_general | solution.py:92
  167.9 2.3 fusion.110
  170.2 8.4 %fusion.114 = (f32[8,512]{1,0:T(8,128)S(1)}, f32[8,512,576]{1,2,0:T(8,128)}) fusion(pred[512,576]{0,1:T(8,128)(4,1)S(1)} %copy-done, bf16[1088,8,16]{0,2,1:T(8,128)(2,1)S(1)} %copy-done.3, s32[]{:T(128)S(6)} %select_n.85, bf16[1024,8,16]{0,2,1:T(8,128)(2,1)} %get-tuple-element.496, s32[]{:T(128)S(6)} %select_n.84), kind=kOutput, calls=%fused_computation.76.clone.1 | convolution fusion | flops 165151296 | bytes 10635264 | tf_op jit(solution)/shard_map/while/body/eval_jaxpr/sub | solution.py:113
  178.6 6.5 %fusion.115 = f32[1,512,8,128]{1,3,2,0:T(8,128)} fusion(f32[8,512,576]{1,2,0:T(8,128)} %get-tuple-element.427, f32[8,512]{1,0:T(8,128)S(1)} %get-tuple-element.428, bf16[1088,8,128]{2,0,1:T(8,128)(2,1)} %get-tuple-element.498, s32[]{:T(128)S(6)} %select_n.85), kind=kOutput, calls=%fused_computation.24.clone.1 | convolution fusion | flops 608698368 | bytes 12730372 | tf_op jit(solution)/shard_map/while/body/eval_jaxpr/hbc,chv->bhv/dot_general | solution.py:115
  194.4 4.6 %fusion.111 = f32[8,128,512]{2,1,0:T(8,128)S(1)} fusion(pred[512,512]{1,0:T(8,128)(4,1)} %iota_compare_fusion.3, bf16[1024,8,128]{2,0,1:T(8,128)(2,1)} %get-tuple-element.495, s32[]{:T(128)S(6)} %select_n.84, bf16[1024,8,16]{0,2,1:T(8,128)(2,1)} %copy-done.1, bf16[1024,8,16]{0,2,1:T(8,128)(2,1)} %get-tuple-element.496), kind=kOutput, calls=%fused_computation.12.clone.1 | convolution fusion | flops 618659840 | bytes 3671552 | tf_op jit(solution)/shard_map/while/body/eval_jaxpr/hbc,chv->bhv/dot_general | solution.py:90
  199.6 3.7 %bitcast_dynamic-update-slice_fusion.2 = f32[2,512,8,128]{1,3,2,0:T(8,128)} fusion(f32[2,512,8,128]{1,3,2,0:T(8,128)} %get-tuple-element.472, s32[]{:T(128)S(6)} %copy.85, f32[8,128,512]{2,1,0:T(8,128)S(1)} %fusion.111, bf16[512,8,256]{0,2,1:T(8,128)(2,1)S(1)} %bitcast.73, bf16[512,8,16]{0,2,1:T(8,128)(2,1)} %multiply_convert_fusion.7, ...), kind=kOutput, calls=%fused_computation.22.clone.1 | convolution fusion | flops 293774336 | bytes 7541286 | tf_op jit(solution)/shard_map/while/body/eval_jaxpr/bhf,hfv->bhv/dot_general | solution.py:92
  203.4 2.3 fusion.110
  205.7 8.4 %fusion.114 = (f32[8,512]{1,0:T(8,128)S(1)}, f32[8,512,576]{1,2,0:T(8,128)}) fusion(pred[512,576]{0,1:T(8,128)(4,1)S(1)} %copy-done, bf16[1088,8,16]{0,2,1:T(8,128)(2,1)S(1)} %copy-done.3, s32[]{:T(128)S(6)} %select_n.85, bf16[1024,8,16]{0,2,1:T(8,128)(2,1)} %get-tuple-element.496, s32[]{:T(128)S(6)} %select_n.84), kind=kOutput, calls=%fused_computation.76.clone.1 | convolution fusion | flops 165151296 | bytes 10635264 | tf_op jit(solution)/shard_map/while/body/eval_jaxpr/sub | solution.py:113
  214.1 6.5 %fusion.115 = f32[1,512,8,128]{1,3,2,0:T(8,128)} fusion(f32[8,512,576]{1,2,0:T(8,128)} %get-tuple-element.427, f32[8,512]{1,0:T(8,128)S(1)} %get-tuple-element.428, bf16[1088,8,128]{2,0,1:T(8,128)(2,1)} %get-tuple-element.498, s32[]{:T(128)S(6)} %select_n.85), kind=kOutput, calls=%fused_computation.24.clone.1 | convolution fusion | flops 608698368 | bytes 12730372 | tf_op jit(solution)/shard_map/while/body/eval_jaxpr/hbc,chv->bhv/dot_general | solution.py:115
  220.6 2.1 copy.71
  224.2 2.8 multiply_reduce_fusion
  227.0 5.3 %copy.52 = f32[2,512,8,128]{3,2,1,0:T(8,128)} copy(f32[2,512,8,128]{1,3,2,0:T(8,128)} %get-tuple-element.272) | data formatting | bytes 8388608 | tf_op jit(solution)/shard_map/while | solution.py:120
  232.5 4.1 %fusion.66 = bf16[1024,8,128]{2,1,0:T(8,128)(2,1)S(1)} fusion(f32[2,512,8,128]{3,2,1,0:T(8,128)} %get-tuple-element.273, f32[2,512,8,128]{3,2,1,0:T(8,128)} %copy.52, f32[8,128]{1,0:T(8,128)S(1)} %bitcast.90, f32[1024,8]{1,0:T(8,128)S(1)} %copy.53), kind=kLoop, calls=%fused_computation.68 | loop fusion | flops 4194304 | bytes 10522624 | tf_op jit(solution)/shard_map/convert_element_type | solution.py:125
  236.6 28.8 %all_to_all.69 = bf16[1024,8,128]{2,1,0:T(8,128)(2,1)S(1)} all-to-all(bf16[1024,8,128]{2,1,0:T(8,128)(2,1)S(1)} %fusion.66), channel_id=1, replica_groups=mesh['groups'=2,'ctx'=4,'head'=4] {'head'}, dimensions={0} | all-to-all | bytes 4194304 | tf_op jit(solution)/shard_map/all_to_all | solution.py:126
  265.4 2.6 copy.55
  268.0 4.1 %copy.56 = bf16[256,4096]{1,0:T(8,128)(2,1)} copy(bf16[256,4096]{0,1:T(8,128)(2,1)} %bitcast.79) | data formatting | bytes 4194304 | tf_op jit(solution)/shard_map/reshape | solution.py:127
  (85 shorter events, 35.4 us)
Async XLA Ops:
  8.3 10.3 %all-to-all-start = ((bf16[256,32,16]{0,2,1:T(8,128)(2,1)}), bf16[256,32,16]{0,2,1:T(8,128)(2,1)S(1)}, u32[]{:S(2)}, u32[]{:S(2)}) async-start(bf16[256,32,16]{0,2,1:T(8,128)(2,1)} %bitcast.7), calls=%async_computation | async-start | bytes 524288 | tf_op jit(solution)/shard_map/all_to_all | solution.py:50
  18.7 29.3 %all-to-all-start.1 = ((bf16[256,32,128]{2,0,1:T(8,128)(2,1)}), bf16[256,32,128]{2,0,1:T(8,128)(2,1)S(1)}, u32[]{:S(2)}, u32[]{:S(2)}) async-start(bf16[256,32,128]{2,0,1:T(8,128)(2,1)} %copy.45), calls=%async_computation.1 | async-start | bytes 4194304 | tf_op jit(solution)/shard_map/all_to_all | solution.py:51
  22.3 123.4 %all-gather.3.cloned.1.call-start = ((), (), s32[]{:S(2)}) async-start(), calls=%async_computation.4 | async-start | bytes 5591040 | tf_op jit(solution)/shard_map/all_gather | solution.py:23
  49.4 5.7 %copy-start.4 = (bf16[256,512]{1,0:T(8,128)(2,1)S(1)}, bf16[256,512]{1,0:T(8,128)(2,1)}, u32[]{:S(2)}) copy-start(bf16[256,512]{1,0:T(8,128)(2,1)} %param.8) | copy-start | bytes 786436
  55.9 9.4 %all-to-all-start.2 = ((bf16[256,32,16]{0,2,1:T(8,128)(2,1)}), bf16[256,32,16]{0,2,1:T(8,128)(2,1)S(1)}, u32[]{:S(2)}, u32[]{:S(2)}) async-start(bf16[256,32,16]{0,2,1:T(8,128)(2,1)} %bitcast.17), calls=%async_computation.2 | async-start | bytes 524288 | tf_op jit(solution)/shard_map/all_to_all | solution.py:49
  59.4 11.9 %collective-permute-start.1 = (bf16[64,8,16]{0,2,1:T(8,128)(2,1)S(1)}, bf16[64,8,16]{0,2,1:T(8,128)(2,1)S(1)}, u32[]{:S(2)}, u32[]{:S(2)}) collective-permute-start(bf16[64,8,16]{0,2,1:T(8,128)(2,1)S(1)} %slice.9), channel_id=1, source_target_pairs={{0,4},{4,8},{8,12},{1,5},{5,9},{9,13},{2,6},{6,10},{10,14},{3,7},{... | collective-permute-start | bytes 49160 | tf_op jit(solution)/shard_map/ppermute | solution.py:18
  67.0 10.3 %collective-permute-start = (bf16[64,8,128]{2,0,1:T(8,128)(2,1)S(1)}, bf16[64,8,128]{2,0,1:T(8,128)(2,1)S(1)}, u32[]{:S(2)}, u32[]{:S(2)}) collective-permute-start(bf16[64,8,128]{2,0,1:T(8,128)(2,1)S(1)} %slice.8), channel_id=1, source_target_pairs={{0,4},{4,8},{8,12},{1,5},{5,9},{9,13},{2,6},{6,10},{10,14},{3,7},{... | collective-permute-start | bytes 393224 | tf_op jit(solution)/shard_map/ppermute | solution.py:18
  153.2 4.6 %copy-start.1 = (bf16[1024,8,16]{0,2,1:T(8,128)(2,1)}, bf16[1024,8,16]{0,2,1:T(8,128)(2,1)S(1)}, u32[]{:S(2)}) copy-start(bf16[1024,8,16]{0,2,1:T(8,128)(2,1)S(1)} %get-tuple-element.497) | copy-start | bytes 786436 | tf_op jit(solution)/shard_map/while
  163.5 4.4 %slice-start = ((s8[4587520]{0:T(1024)(128)(4,1)}), s8[4194304]{0:T(1024)(128)(4,1)S(1)}, s32[]{:S(2)}) async-start(s8[4587520]{0:T(1024)(128)(4,1)} %bitcast.74), calls=%async_computation.5 | async-start | bytes 8388608 | tf_op jit(solution)/shard_map/while
  164.2 3.7 %slice-start.1 = ((s8[4587520]{0:T(1024)(128)(4,1)}), s8[393216]{0:T(1024)(128)(4,1)S(1)}, s32[]{:S(2)}) async-start(s8[4587520]{0:T(1024)(128)(4,1)} %bitcast.74), calls=%async_computation.6 | async-start | bytes 786432 | tf_op jit(solution)/shard_map/while
  167.9 2.3 copy-start
  167.9 2.3 copy-start.3
  185.1 3.6 %copy-start.2 = (bf16[1024,8,16]{0,2,1:T(8,128)(2,1)S(1)}, bf16[1024,8,16]{0,2,1:T(8,128)(2,1)}, u32[]{:S(2)}) copy-start(bf16[1024,8,16]{0,2,1:T(8,128)(2,1)} %copy-done.1) | copy-start | bytes 786436 | tf_op jit(solution)/shard_map/while
  188.7 4.6 %copy-start.1 = (bf16[1024,8,16]{0,2,1:T(8,128)(2,1)}, bf16[1024,8,16]{0,2,1:T(8,128)(2,1)S(1)}, u32[]{:S(2)}) copy-start(bf16[1024,8,16]{0,2,1:T(8,128)(2,1)S(1)} %get-tuple-element.497) | copy-start | bytes 786436 | tf_op jit(solution)/shard_map/while
  198.9 4.4 %slice-start = ((s8[4587520]{0:T(1024)(128)(4,1)}), s8[4194304]{0:T(1024)(128)(4,1)S(1)}, s32[]{:S(2)}) async-start(s8[4587520]{0:T(1024)(128)(4,1)} %bitcast.74), calls=%async_computation.5 | async-start | bytes 8388608 | tf_op jit(solution)/shard_map/while
  199.6 3.7 %slice-start.1 = ((s8[4587520]{0:T(1024)(128)(4,1)}), s8[393216]{0:T(1024)(128)(4,1)S(1)}, s32[]{:S(2)}) async-start(s8[4587520]{0:T(1024)(128)(4,1)} %bitcast.74), calls=%async_computation.6 | async-start | bytes 786432 | tf_op jit(solution)/shard_map/while
  203.4 2.4 copy-start
  203.4 2.4 copy-start.3
  220.6 3.6 %copy-start.2 = (bf16[1024,8,16]{0,2,1:T(8,128)(2,1)S(1)}, bf16[1024,8,16]{0,2,1:T(8,128)(2,1)}, u32[]{:S(2)}) copy-start(bf16[1024,8,16]{0,2,1:T(8,128)(2,1)} %copy-done.1) | copy-start | bytes 786436 | tf_op jit(solution)/shard_map/while
  227.0 5.5 %copy-start.5 = (f32[1024]{0:T(1024)S(1)}, f32[1024]{0:T(1024)}, u32[]{:S(2)}) copy-start(f32[1024]{0:T(1024)} %param.11) | copy-start | bytes 12292
Sparse Core Ops, SparseCore 0:
  55.2 90.4 all-gather.2
where the time goes:
time: 280 us; the launch traced here: 279 us
  waiting for transfers between devices  92.4 us (33%)
  matrix products  55.3 us (20%)
  local copies, waits for them, and re-layouts  39.3 us (14%)
  blocking collectives  28.8 us (10%)
  other arithmetic  28.4 us (10%)
  starting transfers between devices  19.7 us (7%)
  between operations  13.6 us (5%)
    all_gather x1, waiting for transfers between devices, entering(): everything = lax.all_gather(shard, axis)  65.2 us
    all_to_all x1, blocking collectives, per_device(): lax.all_to_all(mixed, 'head', split_axis=0, concat_axis=1, tiled=True)  28.8 us
    all_to_all x1, waiting for transfers between devices, per_device(): lax.all_to_all(value_tok, 'head', split_axis=1, concat_axis=0, tiled=True)  20.3 us
    sub x2, matrix products, block_step(): expo = jnp.where(valid, jnp.exp(window_scores - highest_score), 0.0)  16.7 us
    dot_general x2, matrix products, block_step(): jnp.einsum('hbc,chv->bhv', weights, value_window, preferred_element_type=...  13 us
    dot_general x2, matrix products, block_step(): jnp.einsum('hbc,chv->bhv', kernel, value_block, preferred_element_type=jn...  9.1 us
    ppermute x2, starting transfers between devices, shifted(): return lax.ppermute(shard, axis, pairs)  8.46 us
    dot_general x2, matrix products, block_step(): jnp.einsum('bhf,hfv->bhv', query_feat, state.astype(jnp.bfloat16), prefer...  7.45 us
  transfers between devices with their start and end apart: 6, of which 4 were waited for; matrix products, arithmetic and copies ran while one was open for 6% of the time, Pallas kernels for 0%

commit v1 on v0

--- a/solution.py
+++ b/solution.py
@@ -10,6 +10,28 @@
 WINDOW = 64
 outer_scale = 1.0 / (4.0 * math.sqrt(2.0))
 epsilon = 1e-06
+
+
+def cut_along(array, dim, devices):
+    before, after = (array.shape[:dim], array.shape[dim + 1 :])
+    return jnp.moveaxis(array.reshape(*before, devices, -1, *after), dim, 0)
+
+
+def joined_along(blocks, dim):
+    shape = list(blocks.shape[1:])
+    shape[dim] *= blocks.shape[0]
+    return jnp.moveaxis(blocks, 0, dim).reshape(shape)
+
+
+def sent_to_each(x, axis, split_dim, concat_dim):
+    peers, position = (lax.axis_size(axis), lax.axis_index(axis))
+    blocks = cut_along(x, split_dim, peers)
+    finished = [blocks[position]]
+    for step in range(1, peers):
+        sent = blocks[(position + step) % peers]
+        finished.append(lax.ppermute(sent, axis, [(i, (i + step) % peers) for i in range(peers)]))
+    blocks = jnp.stack(finished)[(position - jnp.arange(peers)) % peers]
+    return joined_along(blocks, concat_dim)
 
 
 def shifted(shard, axis, by):
@@ -123,7 +145,7 @@
     scale = lax.rsqrt(jnp.mean(linear * linear, axis=2, keepdims=True) + epsilon)
     gains = gain.reshape(heads_here, VD)
     mixed = (linear * scale * gains + window).astype(jnp.bfloat16)
-    tokens_back = lax.all_to_all(mixed, "head", split_axis=0, concat_axis=1, tiled=True)
+    tokens_back = sent_to_each(mixed, "head", 0, 1)
     return tokens_back.reshape(tokens_back.shape[0], HEADS * VD)
 
 

time: 280 us -> 268 us (0.957)
  blocking collectives: 28.8 us -> 0 us
  waiting for transfers between devices: 92.4 us -> 117 us
  matrix products: 55.3 us -> 48.4 us
  other arithmetic: 28.4 us -> 21.7 us
  local copies, waits for them, and re-layouts: 39.3 us -> 42.8 us
    all_to_all x1 -> x0, blocking collectives: 28.8 us -> none  [per_device(): lax.all_to_all(mixed, 'head', split_axis=0, concat_axis=1, tiled=True)]
    ppermute x0 -> x3, waiting for transfers between devices: none -> 23.7 us  [sent_to_each(): lax.ppermute(sent, axis, [(i, (i + step) % peers) for i in range(peers)])]
    reshape x1 -> x0, local copies, waits for them, and re-layouts: 4.06 us -> none  [per_device(): return tokens_back.reshape(tokens_back.shape[0], HEADS * VD)]
    transpose x0 -> x1, local copies, waits for them, and re-layouts: none -> 2.99 us  [joined_along(): return jnp.moveaxis(blocks, 0, dim).reshape(shape)]
    another operation x0 -> x1, local copies, waits for them, and re-layouts: none -> 2.86 us  [per_device(): return tokens_back.reshape(tokens_back.shape[0], HEADS * VD)]
    another operation x8 -> x9, other arithmetic: 5.83 us -> 2.99 us
    unnamed x7 -> x15, local copies, waits for them, and re-layouts: 5.9 us -> 7.95 us
  transfers between devices with their start and end apart: 6 -> 9, of which waited for: 4 -> 6; matrix products, arithmetic and copies ran while one was open for 6% -> 6% of each run, Pallas kernels for 0% -> 0%
where the time goes in v1:
time: 268 us; the launch traced here: 267 us
  waiting for transfers between devices  117 us (44%)
  matrix products  48.4 us (18%)
  local copies, waits for them, and re-layouts  42.8 us (16%)
  starting transfers between devices  21.7 us (8%)
  other arithmetic  21.7 us (8%)
  between operations  13.7 us (5%)
    all_gather x1, waiting for transfers between devices, entering(): everything = lax.all_gather(shard, axis)  67.5 us
    ppermute x3, waiting for transfers between devices, sent_to_each(): lax.ppermute(sent, axis, [(i, (i + step) % peers) for i in range(peers)])  23.7 us
    all_to_all x1, waiting for transfers between devices, per_device(): lax.all_to_all(value_tok, 'head', split_axis=1, concat_axis=0, tiled=True)  20.3 us
    sub x2, matrix products, block_step(): expo = jnp.where(valid, jnp.exp(window_scores - highest_score), 0.0)  14.9 us
    dot_general x2, matrix products, block_step(): jnp.einsum('hbc,chv->bhv', weights, value_window, preferred_element_type=...  13 us
    dot_general x2, matrix products, block_step(): jnp.einsum('hbc,chv->bhv', kernel, value_block, preferred_element_type=jn...  9.04 us
    ppermute x2, starting transfers between devices, shifted(): return lax.ppermute(shard, axis, pairs)  8.45 us
    unnamed x15, local copies, waits for them, and re-layouts  7.95 us
  transfers between devices with their start and end apart: 9, of which 6 were waited for; matrix products, arithmetic and copies ran while one was open for 6% of the time, Pallas kernels for 0%

profile of v1, /device:TPU:0, one launch (start us, length us, event | category | flops | bytes accessed | tf_op | source)
XLA Modules:
  0.0 266.7 jit_solution(3608715375270540987)
XLA Ops:
  8.3 4.2 %all-to-all-start = ((bf16[256,32,16]{0,2,1:T(8,128)(2,1)}), bf16[256,32,16]{0,2,1:T(8,128)(2,1)S(1)}, u32[]{:S(2)}, u32[]{:S(2)}) async-start(bf16[256,32,16]{0,2,1:T(8,128)(2,1)} %bitcast.7), calls=%async_computation | async-start | bytes 524288 | tf_op jit(solution)/shard_map/all_to_all | solution.py:72
  12.5 3.3 %copy.44 = bf16[256,4096]{0,1:T(8,128)(2,1)S(1)} copy(bf16[256,4096]{1,0:T(8,128)(2,1)} %param.10) | data formatting | bytes 4194304 | tf_op args[2]
  15.8 2.9 %copy.45 = bf16[256,32,128]{2,0,1:T(8,128)(2,1)} copy(bf16[256,32,128]{0,2,1:T(8,128)(2,1)S(1)} %bitcast.87) | data formatting | bytes 4194304 | tf_op jit(solution)/shard_map/reshape | solution.py:69
  18.7 3.6 %all-to-all-start.1 = ((bf16[256,32,128]{2,0,1:T(8,128)(2,1)}), bf16[256,32,128]{2,0,1:T(8,128)(2,1)S(1)}, u32[]{:S(2)}, u32[]{:S(2)}) async-start(bf16[256,32,128]{2,0,1:T(8,128)(2,1)} %copy.45), calls=%async_computation.1 | async-start | bytes 4194304 | tf_op jit(solution)/shard_map/all_to_all | solution.py:73
  23.8 3.8 %pad_maximum_fusion = bf16[1024,8,273]{0,2,1:T(8,128)(2,1)} fusion(bf16[1024,8,256]{0,2,1:T(8,128)(2,1)S(1)} %bitcast.82, bf16[1024,8,16]{0,2,1:T(8,128)(2,1)S(1)} %multiply_convert_fusion.3, bf16[273]{0:T(512)(128)(2,1)S(1)} %pad.11.clone), kind=kLoop, calls=%fused_computation.67 | loop fusion | flops 13418496 | bytes 8929826 | tf_op jit(solution)/shard_map/concatenate | solution.py:62
  27.6 20.3 %all-to-all-done.1 = bf16[256,32,128]{2,0,1:T(8,128)(2,1)S(1)} async-done(((bf16[256,32,128]{2,0,1:T(8,128)(2,1)}), bf16[256,32,128]{2,0,1:T(8,128)(2,1)S(1)}, u32[]{:S(2)}, u32[]{:S(2)}) %all-to-all-start.1) | async-done | bytes 2097184 | tf_op jit(solution)/shard_map/all_to_all | solution.py:73
  51.0 4.4 %fusion.77 = f32[8,273,128]{2,1,0:T(8,128)S(1)} fusion(bf16[1024,8,273]{0,2,1:T(8,128)(2,1)} %pad_maximum_fusion, bf16[1024,8,128]{2,0,1:T(8,128)(2,1)S(1)} %bitcast.77), kind=kOutput, calls=%fused_computation.87 | convolution fusion | flops 572522496 | bytes 7688192 | tf_op jit(solution)/shard_map/bhf,bhv->hfv/dot_general | solution.py:86
  57.6 3.4 %all-to-all-start.2 = ((bf16[256,32,16]{0,2,1:T(8,128)(2,1)}), bf16[256,32,16]{0,2,1:T(8,128)(2,1)S(1)}, u32[]{:S(2)}, u32[]{:S(2)}) async-start(bf16[256,32,16]{0,2,1:T(8,128)(2,1)} %bitcast.17), calls=%async_computation.2 | async-start | bytes 524288 | tf_op jit(solution)/shard_map/all_to_all | solution.py:71
  61.7 4.1 %collective-permute-start.1 = (bf16[64,8,16]{0,2,1:T(8,128)(2,1)}, bf16[64,8,16]{0,2,1:T(8,128)(2,1)S(1)}, u32[]{:S(2)}, u32[]{:S(2)}) collective-permute-start(bf16[64,8,16]{0,2,1:T(8,128)(2,1)} %slice.11), channel_id=1, source_target_pairs={{0,4},{4,8},{8,12},{1,5},{5,9},{9,13},{2,6},{6,10},{10,14},{3,7},{... | collective-permute-start | bytes 49160 | tf_op jit(solution)/shard_map/ppermute | solution.py:40
  68.7 4.3 %collective-permute-start = (bf16[64,8,128]{2,0,1:T(8,128)(2,1)S(1)}, bf16[64,8,128]{2,0,1:T(8,128)(2,1)S(1)}, u32[]{:S(2)}, u32[]{:S(2)}) collective-permute-start(bf16[64,8,128]{2,0,1:T(8,128)(2,1)S(1)} %slice.10), channel_id=1, source_target_pairs={{0,4},{4,8},{8,12},{1,5},{5,9},{9,13},{2,6},{6,10},{10,14},{3,7},{... | collective-permute-start | bytes 393224 | tf_op jit(solution)/shard_map/ppermute | solution.py:40
  74.9 4.2 %collective-permute-done = bf16[64,8,128]{2,0,1:T(8,128)(2,1)S(1)} collective-permute-done((bf16[64,8,128]{2,0,1:T(8,128)(2,1)S(1)}, bf16[64,8,128]{2,0,1:T(8,128)(2,1)S(1)}, u32[]{:S(2)}, u32[]{:S(2)}) %collective-permute-start) | collective-permute-done | bytes 131104 | tf_op jit(solution)/shard_map/ppermute | solution.py:40
  80.6 67.5 %all-gather.3.cloned.1.call-done = f32[32,273,128]{2,0,1:T(8,128)} async-done(((f32[8,273,128]{2,0,1:T(8,128)}), f32[32,273,128]{2,0,1:T(8,128)}) %all-gather.3.cloned.1.call-update) | async-done | bytes 4472848 | tf_op jit(solution)/shard_map/all_gather | solution.py:45
  148.1 7.5 %while.32 = (s32[]{:T(128)}, f32[8,273,128]{2,1,0:T(8,128)S(1)}, s32[]{:T(128)}, f32[4,8,273,128]{3,1,0,2:T(8,128)}, s32[]{:T(128)}, /*index=5*/s32[]{:T(128)}) while((s32[]{:T(128)}, f32[8,273,128]{2,1,0:T(8,128)S(1)}, s32[]{:T(128)}, f32[4,8,273,128]{3,1,0,2:T(8,128)}, s32[]{:T(128)}, /*index=5*/s32[]{:T(128)}) %tuple.74), condition=%wide.region_1.2_spmd.clone, body=%wide.region_0.1_spmd.clone.sunk | while | flops 838660 | bytes 5591141 | solution.py:53
  155.6 57.8 %while.31 = (s32[]{:T(128)}, f32[8,273,128]{2,1,0:T(8,128)S(1)}, f32[2,512,8,128]{1,3,2,0:T(8,128)}, f32[2,512,8,128]{3,2,1,0:T(8,128)}, s32[2]{0:T(128)S(1)}, /...) while((s32[]{:T(128)}, f32[8,273,128]{2,1,0:T(8,128)S(1)}, ...), condition=%wide.region_5.6_spmd, body=%wide.region_2.5_spmd.sunk | while | flops 1977677568 | bytes 75423312 | solution.py:142
  157.7 4.5 %fusion.111 = f32[8,128,512]{2,1,0:T(8,128)S(1)} fusion(pred[512,512]{1,0:T(8,128)(4,1)} %iota_compare_fusion.3, bf16[1024,8,128]{2,0,1:T(8,128)(2,1)} %get-tuple-element.499, s32[]{:T(128)S(6)} %select_n.151, bf16[1024,8,16]{0,2,1:T(8,128)(2,1)} %get-tuple-element.501, bf16[1024,8,16]{0,2,1:T(8,128)(2,1)S(1)} %get-tuple-element.500), kind=kOutput, calls=%fused_computation.13.clone.1 | convolution fusion | flops 618659840 | bytes 3671552 | tf_op jit(solution)/shard_map/while/body/eval_jaxpr/hbc,chv->bhv/dot_general | solution.py:112
  163.0 2.5 bitcast_dynamic-update-slice_fusion.2
  167.0 7.4 %fusion.114 = (f32[8,512]{1,0:T(8,128)S(1)}, f32[8,512,576]{1,2,0:T(8,128)}) fusion(pred[512,576]{0,1:T(8,128)(4,1)S(1)} %fusion.113, bf16[1088,8,16]{0,2,1:T(8,128)(2,1)S(1)} %copy-done.5, s32[]{:T(128)S(6)} %select_n.152, bf16[1024,8,16]{0,2,1:T(8,128)(2,1)S(1)} %get-tuple-element.500, s32[]{:T(128)S(6)} %select_n.151), kind=kOutput, calls=%fused_computation.86.clone.1 | convolution fusion | flops 165151296 | bytes 10635264 | tf_op jit(solution)/shard_map/while/body/eval_jaxpr/sub | solution.py:135
  174.4 6.5 %fusion.115 = f32[1,512,8,128]{1,3,2,0:T(8,128)} fusion(f32[8,512,576]{1,2,0:T(8,128)} %get-tuple-element.431, f32[8,512]{1,0:T(8,128)S(1)} %get-tuple-element.432, bf16[1088,8,128]{2,0,1:T(8,128)(2,1)} %get-tuple-element.502, s32[]{:T(128)S(6)} %select_n.152), kind=kOutput, calls=%fused_computation.25.clone.1 | convolution fusion | flops 608698368 | bytes 12730372 | tf_op jit(solution)/shard_map/while/body/eval_jaxpr/hbc,chv->bhv/dot_general | solution.py:137
  180.9 2.1 copy.71
  186.6 4.5 %fusion.111 = f32[8,128,512]{2,1,0:T(8,128)S(1)} fusion(pred[512,512]{1,0:T(8,128)(4,1)} %iota_compare_fusion.3, bf16[1024,8,128]{2,0,1:T(8,128)(2,1)} %get-tuple-element.499, s32[]{:T(128)S(6)} %select_n.151, bf16[1024,8,16]{0,2,1:T(8,128)(2,1)} %get-tuple-element.501, bf16[1024,8,16]{0,2,1:T(8,128)(2,1)S(1)} %get-tuple-element.500), kind=kOutput, calls=%fused_computation.13.clone.1 | convolution fusion | flops 618659840 | bytes 3671552 | tf_op jit(solution)/shard_map/while/body/eval_jaxpr/hbc,chv->bhv/dot_general | solution.py:112
  191.9 2.5 bitcast_dynamic-update-slice_fusion.2
  195.9 7.4 %fusion.114 = (f32[8,512]{1,0:T(8,128)S(1)}, f32[8,512,576]{1,2,0:T(8,128)}) fusion(pred[512,576]{0,1:T(8,128)(4,1)S(1)} %fusion.113, bf16[1088,8,16]{0,2,1:T(8,128)(2,1)S(1)} %copy-done.5, s32[]{:T(128)S(6)} %select_n.152, bf16[1024,8,16]{0,2,1:T(8,128)(2,1)S(1)} %get-tuple-element.500, s32[]{:T(128)S(6)} %select_n.151), kind=kOutput, calls=%fused_computation.86.clone.1 | convolution fusion | flops 165151296 | bytes 10635264 | tf_op jit(solution)/shard_map/while/body/eval_jaxpr/sub | solution.py:135
  203.3 6.5 %fusion.115 = f32[1,512,8,128]{1,3,2,0:T(8,128)} fusion(f32[8,512,576]{1,2,0:T(8,128)} %get-tuple-element.431, f32[8,512]{1,0:T(8,128)S(1)} %get-tuple-element.432, bf16[1088,8,128]{2,0,1:T(8,128)(2,1)} %get-tuple-element.502, s32[]{:T(128)S(6)} %select_n.152), kind=kOutput, calls=%fused_computation.25.clone.1 | convolution fusion | flops 608698368 | bytes 12730372 | tf_op jit(solution)/shard_map/while/body/eval_jaxpr/hbc,chv->bhv/dot_general | solution.py:137
  209.9 2.1 copy.71
  213.4 5.2 %copy.52 = f32[2,512,8,128]{3,2,1,0:T(8,128)} copy(f32[2,512,8,128]{1,3,2,0:T(8,128)} %get-tuple-element.272) | data formatting | bytes 8388608 | tf_op jit(solution)/shard_map/while | solution.py:142
  218.7 2.8 %multiply_reduce_fusion = f32[2,512,8]{1,2,0:T(8,128)S(1)} fusion(f32[2,512,8,128]{1,3,2,0:T(8,128)} %get-tuple-element.272), kind=kLoop, calls=%fused_computation.69 | loop fusion | flops 2088960 | bytes 4227072 | tf_op jit(solution)/shard_map/reduce_sum | solution.py:145
  221.7 4.1 %add_convert_fusion = bf16[4,256,8,128]{3,2,1,0:T(8,128)(2,1)S(1)} fusion(f32[4,256,8,128]{3,2,1,0:T(8,128)} %bitcast.94, f32[4,256,8,128]{3,2,1,0:T(8,128)} %bitcast.81, f32[8,128]{1,0:T(8,128)S(1)} %bitcast.101, f32[4,256,8]{2,1,0:T(8,128)S(1)} %copy.53), kind=kLoop, calls=%fused_computation.68 | loop fusion | flops 4194304 | bytes 10522624 | tf_op jit(solution)/shard_map/convert_element_type | solution.py:147
  227.9 11.7 %collective-permute-done.4 = bf16[256,8,128]{2,1,0:T(8,128)(2,1)S(1)} collective-permute-done((bf16[256,8,128]{2,1,0:T(8,128)(2,1)S(1)}, bf16[256,8,128]{2,1,0:T(8,128)(2,1)S(1)}, u32[]{:S(2)}, u32[]{:S(2)}) %collective-permute-start.4) | collective-permute-done | bytes 524320 | tf_op jit(solution)/shard_map/ppermute | solution.py:32
  239.6 12.0 %collective-permute-done.3 = bf16[256,8,128]{2,1,0:T(8,128)(2,1)S(1)} collective-permute-done((bf16[256,8,128]{2,1,0:T(8,128)(2,1)S(1)}, bf16[256,8,128]{2,1,0:T(8,128)(2,1)S(1)}, u32[]{:S(2)}, u32[]{:S(2)}) %collective-permute-start.3) | collective-permute-done | bytes 524320 | tf_op jit(solution)/shard_map/ppermute | solution.py:32
  251.9 2.1 gather_fusion
  254.0 3.0 %copy.55 = bf16[256,4,8,128]{0,3,2,1:T(8,128)(2,1)S(1)} copy(bf16[256,4,8,128]{3,2,0,1:T(8,128)(2,1)} %bitcast.85) | data formatting | bytes 4194304 | tf_op jit(solution)/shard_map/transpose | solution.py:23
  257.0 2.9 %copy.56 = bf16[256,4096]{1,0:T(8,128)(2,1)} copy(bf16[256,4096]{0,1:T(8,128)(2,1)S(1)} %bitcast.86) | data formatting | bytes 4194304 | tf_op jit(solution)/shard_map/reshape;reshape | solution.py:149
  (95 shorter events, 35.3 us)
Async XLA Ops:
  8.3 10.3 %all-to-all-start = ((bf16[256,32,16]{0,2,1:T(8,128)(2,1)}), bf16[256,32,16]{0,2,1:T(8,128)(2,1)S(1)}, u32[]{:S(2)}, u32[]{:S(2)}) async-start(bf16[256,32,16]{0,2,1:T(8,128)(2,1)} %bitcast.7), calls=%async_computation | async-start | bytes 524288 | tf_op jit(solution)/shard_map/all_to_all | solution.py:72
  18.7 29.3 %all-to-all-start.1 = ((bf16[256,32,128]{2,0,1:T(8,128)(2,1)}), bf16[256,32,128]{2,0,1:T(8,128)(2,1)S(1)}, u32[]{:S(2)}, u32[]{:S(2)}) async-start(bf16[256,32,128]{2,0,1:T(8,128)(2,1)} %copy.45), calls=%async_computation.1 | async-start | bytes 4194304 | tf_op jit(solution)/shard_map/all_to_all | solution.py:73
  22.3 125.8 %all-gather.3.cloned.1.call-start = ((), (), s32[]{:S(2)}) async-start(), calls=%async_computation.3 | async-start | bytes 5591040 | tf_op jit(solution)/shard_map/all_gather | solution.py:45
  22.4 38.6 %copy-start.3 = (bf16[4,8,2,8,256]{4,3,0,2,1:T(8,128)(2,1)}, bf16[4,8,2,8,256]{4,3,0,2,1:T(8,128)(2,1)S(1)}, u32[]{:S(2)}) copy-start(bf16[4,8,2,8,256]{4,3,0,2,1:T(8,128)(2,1)S(1)} %copy.64) | copy-start | bytes 786436
  48.0 1.3 copy-start.2
  51.0 28.0 %copy-start = (bf16[4,256,8,128]{3,1,0,2:T(8,128)(2,1)}, bf16[4,256,8,128]{3,1,0,2:T(8,128)(2,1)S(1)}, u32[]{:S(2)}) copy-start(bf16[4,256,8,128]{3,1,0,2:T(8,128)(2,1)S(1)} %copy.47) | copy-start | bytes 6291460
  51.0 5.7 %copy-start.6 = (bf16[256,512]{1,0:T(8,128)(2,1)S(1)}, bf16[256,512]{1,0:T(8,128)(2,1)}, u32[]{:S(2)}) copy-start(bf16[256,512]{1,0:T(8,128)(2,1)} %param.8) | copy-start | bytes 786436
  57.6 9.4 %all-to-all-start.2 = ((bf16[256,32,16]{0,2,1:T(8,128)(2,1)}), bf16[256,32,16]{0,2,1:T(8,128)(2,1)S(1)}, u32[]{:S(2)}, u32[]{:S(2)}) async-start(bf16[256,32,16]{0,2,1:T(8,128)(2,1)} %bitcast.17), calls=%async_computation.2 | async-start | bytes 524288 | tf_op jit(solution)/shard_map/all_to_all | solution.py:71
  61.7 11.4 %collective-permute-start.1 = (bf16[64,8,16]{0,2,1:T(8,128)(2,1)}, bf16[64,8,16]{0,2,1:T(8,128)(2,1)S(1)}, u32[]{:S(2)}, u32[]{:S(2)}) collective-permute-start(bf16[64,8,16]{0,2,1:T(8,128)(2,1)} %slice.11), channel_id=1, source_target_pairs={{0,4},{4,8},{8,12},{1,5},{5,9},{9,13},{2,6},{6,10},{10,14},{3,7},{... | collective-permute-start | bytes 49160 | tf_op jit(solution)/shard_map/ppermute | solution.py:40
  67.0 0.7 copy-start.4
  68.7 10.3 %collective-permute-start = (bf16[64,8,128]{2,0,1:T(8,128)(2,1)S(1)}, bf16[64,8,128]{2,0,1:T(8,128)(2,1)S(1)}, u32[]{:S(2)}, u32[]{:S(2)}) collective-permute-start(bf16[64,8,128]{2,0,1:T(8,128)(2,1)S(1)} %slice.10), channel_id=1, source_target_pairs={{0,4},{4,8},{8,12},{1,5},{5,9},{9,13},{2,6},{6,10},{10,14},{3,7},{... | collective-permute-start | bytes 393224 | tf_op jit(solution)/shard_map/ppermute | solution.py:40
  162.3 3.3 %slice-start = ((s8[4587520]{0:T(1024)(128)(4,1)}), s8[4194304]{0:T(1024)(128)(4,1)S(1)}, s32[]{:S(2)}) async-start(s8[4587520]{0:T(1024)(128)(4,1)} %bitcast.75), calls=%async_computation.4 | async-start | bytes 8388608 | tf_op jit(solution)/shard_map/while
  163.0 2.6 copy-start.1
  163.0 2.5 slice-start.1
  165.5 1.4 copy-start.5
  191.2 3.3 %slice-start = ((s8[4587520]{0:T(1024)(128)(4,1)}), s8[4194304]{0:T(1024)(128)(4,1)S(1)}, s32[]{:S(2)}) async-start(s8[4587520]{0:T(1024)(128)(4,1)} %bitcast.75), calls=%async_computation.4 | async-start | bytes 8388608 | tf_op jit(solution)/shard_map/while
  191.8 2.6 copy-start.1
  191.9 2.5 slice-start.1
  194.4 1.5 copy-start.5
  218.7 3.0 %copy-start.7 = (f32[1024]{0:T(1024)S(1)}, f32[1024]{0:T(1024)}, u32[]{:S(2)}) copy-start(f32[1024]{0:T(1024)} %param.11) | copy-start | bytes 12292
  226.0 13.7 %collective-permute-start.4 = (bf16[256,8,128]{2,1,0:T(8,128)(2,1)S(1)}, bf16[256,8,128]{2,1,0:T(8,128)(2,1)S(1)}, u32[]{:S(2)}, u32[]{:S(2)}) collective-permute-start(bf16[256,8,128]{2,1,0:T(8,128)(2,1)S(1)} %get-tuple-element.332), channel_id=1, source_target_pairs={{0,3},{1,0},{2,1},{3,2},{4,7},{5,4},{6,5},{7,6},{8,11},{9,8},{10,9... | collective-permute-start | bytes 1572872 | tf_op jit(solution)/shard_map/ppermute | solution.py:32
  227.3 24.3 %collective-permute-start.3 = (bf16[256,8,128]{2,1,0:T(8,128)(2,1)S(1)}, bf16[256,8,128]{2,1,0:T(8,128)(2,1)S(1)}, u32[]{:S(2)}, u32[]{:S(2)}) collective-permute-start(bf16[256,8,128]{2,1,0:T(8,128)(2,1)S(1)} %get-tuple-element.333), channel_id=1, source_target_pairs={{0,2},{1,3},{2,0},{3,1},{4,6},{5,7},{6,4},{7,5},{8,10},{9,11},{10,... | collective-permute-start | bytes 1572872 | tf_op jit(solution)/shard_map/ppermute | solution.py:32
  227.7 23.8 %collective-permute-start.2 = (bf16[256,8,128]{2,1,0:T(8,128)(2,1)S(1)}, bf16[256,8,128]{2,1,0:T(8,128)(2,1)S(1)}, u32[]{:S(2)}, u32[]{:S(2)}) collective-permute-start(bf16[256,8,128]{2,1,0:T(8,128)(2,1)S(1)} %get-tuple-element.334), channel_id=1, source_target_pairs={{0,1},{1,2},{2,3},{3,0},{4,5},{5,6},{6,7},{7,4},{8,9},{9,10},{10,1... | collective-permute-start | bytes 1572872 | tf_op jit(solution)/shard_map/ppermute | solution.py:32
Sparse Core Ops, SparseCore 0:
  56.8 91.1 all-gather.2
